TPU v7x, 128 devices: a whole 4x4x4 slice. The times are simulated.
128 devices in a mesh: dp: 32 (over y, x, core), blk: 4 (over z).
Axes of the slice: x: 4, y: 4, z: 4, core: 2. Of those that a mesh axis runs over, the one named last changes fastest.
Arguments:
- prod_feat: bfloat16 [32, 3072, 768], P('dp', 'blk'), may hold values from -23 to 23
- prec_feat: bfloat16 [32, 3072, 768], P('dp', 'blk'), may hold values from -23 to 23
- matched: int32 [32, 3072], P('dp', 'blk'), may hold values from 0 to 3071, each once within a row
- row_weight: float32 [32, 3072], P('dp', 'blk'), may hold values from 0.2 to 28, as said below
- proj_prod: bfloat16 [768, 1024], replicated, may hold values from -0.21875 to 0.21875
- proj_prec: bfloat16 [768, 1024], replicated, may hold values from -0.21875 to 0.21875
Outputs:
- loss_value: float32 [], replicated
- grad_prod: float32 [768, 1024], P('dp', 'blk')
- grad_prec: float32 [768, 1024], P('dp', 'blk')
Inputs may be any that keep to these rules, and one draw needn't show every extreme that they name: `matched`: in each of the 32 groups the 3072 values are a permutation of 0 to 3071. `row_weight`: positive.
All inputs are finite; a program needn't handle non-finite values.
Results may differ from a plain program's by a relative error of at most 0.0027.
Values may be sent and summed in bfloat16 or wider, within the bound.
No kernel may reach another device: no remote copies, remote signals or barrier semaphores. Data moves between devices by JAX's collectives and lax.ppermute only.
A program may use at most 128 MiB of HBM per device.

v0:
```python
import jax
import jax.numpy as jnp
from jax import lax
from jax.sharding import PartitionSpec as P

EPS = 1e-06
LOGIT_SCALE = 50.0


def embed_rows(features, weight):
    projected_raw = jnp.dot(features, weight, preferred_element_type=jnp.float32)
    radius = jnp.sqrt(jnp.sum(projected_raw * projected_raw, axis=1, keepdims=True) + EPS)
    unit_vec = projected_raw / radius
    return (unit_vec, unit_vec.astype(jnp.bfloat16), radius)


def similarity(queries, key_rows):
    return LOGIT_SCALE * lax.dot_general(
        queries, key_rows, (((1,), (1,)), ((), ())), preferred_element_type=jnp.float32
    )


def coefficient(scores, matches, weights, totals):
    probability = jnp.exp(scores - LOGIT_SCALE) / totals[:, None]
    return (weights[:, None] * (probability - matches.astype(jnp.float32))).astype(jnp.bfloat16)


def back_norm(unit_vec, radius, gradient):
    projected = jnp.sum(unit_vec * gradient, axis=1, keepdims=True)
    return ((gradient - unit_vec * projected) / radius).astype(jnp.bfloat16)


def spread_blocks(head, dp_size, blk_size):
    feat, embed = head.shape
    tiles = head.reshape(dp_size, feat // dp_size, blk_size, embed // blk_size)
    tiles = tiles.transpose(0, 2, 1, 3)
    return tiles.reshape(dp_size * blk_size * (feat // dp_size), embed // blk_size)


def per_device(prod_feat, prec_feat, matched, row_weight, proj_prod, proj_prec):
    feat_prod = prod_feat[0]
    feat_prec = prec_feat[0]
    targets = matched[0]
    weights = row_weight[0]
    dp_size = lax.axis_size("dp")
    blk_size = lax.axis_size("blk")
    unit_prod, unit16_prod, radius_prod = embed_rows(feat_prod, proj_prod)
    feat_prec_all = lax.all_gather(feat_prec, "blk", axis=0, tiled=True)
    unit_prec, unit16_prec, radius_prec = embed_rows(feat_prec_all, proj_prec)
    scores = similarity(unit16_prod, unit16_prec)
    columns = lax.iota(jnp.int32, unit16_prec.shape[0])
    matches = targets[:, None] == columns[None, :]
    totals = jnp.sum(jnp.exp(scores - LOGIT_SCALE), axis=1)
    positive = jnp.sum(jnp.where(matches, scores, 0.0), axis=1)
    losses = LOGIT_SCALE + jnp.log(totals) - positive
    loss_local = jnp.sum(weights * losses)
    weight_local = jnp.sum(weights)
    loss_sum, weight_total = lax.psum((loss_local, weight_local), ("dp", "blk"))
    coeffs = coefficient(scores, matches, weights, totals)
    grad_unit_prod = LOGIT_SCALE * jnp.dot(coeffs, unit16_prec, preferred_element_type=jnp.float32)
    grad_prec_part = LOGIT_SCALE * lax.dot_general(
        coeffs, unit16_prod, (((0,), (0,)), ((), ())), preferred_element_type=jnp.float32
    )
    dir_prod = back_norm(unit_prod, radius_prod, grad_unit_prod)
    dir_prec = back_norm(unit_prec, radius_prec, grad_prec_part)
    head_prod = lax.dot_general(
        feat_prod, dir_prod, (((0,), (0,)), ((), ())), preferred_element_type=jnp.float32
    )
    head_prec = lax.dot_general(
        feat_prec_all, dir_prec, (((0,), (0,)), ((), ())), preferred_element_type=jnp.float32
    )
    summed_prod = lax.psum_scatter(
        spread_blocks(head_prod, dp_size, blk_size), ("dp", "blk"), scatter_dimension=0, tiled=True
    )
    summed_prec = lax.psum_scatter(
        spread_blocks(head_prec, dp_size, blk_size), ("dp", "blk"), scatter_dimension=0, tiled=True
    )
    return (loss_sum / weight_total, summed_prod / weight_total, summed_prec / weight_total)


def solution(mesh):
    placed = (P("dp", "blk", None), P("dp", "blk", None), P("dp", "blk"), P("dp", "blk"), P(), P())
    return jax.shard_map(
        per_device,
        mesh=mesh,
        in_specs=placed,
        out_specs=(P(), P("dp", "blk"), P("dp", "blk")),
        check_vma=False,
    )
```

profile of v0, /device:TPU:0, one launch (start us, length us, event | category | flops | bytes accessed | tf_op | source)
XLA Modules:
  0.0 556.1 jit_solution(3797390125440202433)
XLA Ops:
  7.2 0.0 copy-start
  7.2 0.0 all-gather.3.cloned.1.call-start
  7.2 0.7 all-gather.3.cloned.1.call-update
  7.9 0.0 reduce-scatter.3.cloned.1.call-start
  8.0 0.7 reduce.2
  8.7 1.3 fusion.20
  10.0 4.8 multiply_reduce_fusion.3
  14.8 50.2 %all-gather.3.cloned.1.call-done = bf16[1,3072,768]{2,1,0:T(8,128)(2,1)} async-done(((bf16[1,768,768]{2,1,0:T(8,128)(2,1)}), bf16[1,3072,768]{2,1,0:T(8,128)(2,1)}) %all-gather.3.cloned.1.call-update) | async-done | bytes 4718608 | tf_op jit(solution)/shard_map/all_gather | solution.py:48
  65.0 0.0 copy-done
  65.0 0.0 copy-start.3
  65.0 7.4 %multiply_reduce_fusion.1 = (f32[3072]{0:T(1024)S(1)}, f32[3072,1024]{0,1:T(8,128)S(1)}) fusion(bf16[768,1024]{1,0:T(8,128)(2,1)S(1)} %copy-done, bf16[1,3072,768]{2,1,0:T(8,128)(2,1)} %all-gather.3.cloned.1.call-done), kind=kOutput, calls=%fused_computation.2 | convolution fusion | flops 4838126592 | bytes 18886656 | tf_op jit(solution)/shard_map/dot_general | solution.py:11
  72.4 0.0 copy-start.4
  72.4 0.0 copy-done.3
  72.4 9.7 %fusion = (f32[768]{0:T(1024)S(1)}, f32[768]{0:T(1024)S(1)}, f32[768,3072]{1,0:T(8,128)}) fusion(s32[768]{0:T(1024)S(1)} %reduce.2, f32[3072,1024]{0,1:T(8,128)S(1)} %get-tuple-element.12, f32[3072]{0:T(1024)S(1)} %add_sqrt_fusion, f32[768,1024]{1,0:T(8,128)S(1)} %copy-done.3, f32[768]{0:T(1024)S(1)} %add_sqrt_fusion.1), kind=kOutput, calls=%fused_computation.7 | convolution fusion | flops 4853856256 | bytes 25190400 | tf_op jit(solution)/shard_map/dot_general | solution.py:18
  82.2 0.0 copy-done.4
  82.2 13.6 %multiply_reduce_fusion.2 = (f32[768]{0:T(1024)S(1)}, f32[768,1024]{1,0:T(8,128)S(1)}) fusion(f32[768,1024]{1,0:T(8,128)S(1)} %copy-done.3, f32[768]{0:T(1024)S(1)} %add_sqrt_fusion.1, f32[3072,1024]{0,1:T(8,128)} %copy-done.4, f32[3072]{0:T(1024)S(1)} %add_sqrt_fusion, f32[768,3072]{1,0:T(8,128)} %get-tuple-element.13, f32[768]{0:T(1024)S(1)} %get-tuple-element.3, ...), kind=kOutput, calls=%fused_computation.14 | convolution fusion | flops 4860148736 | bytes 28339200 | tf_op jit(solution)/shard_map/dot_general | solution.py:60
  95.7 0.0 copy-start.2
  95.7 15.1 %multiply_reduce_fusion = (f32[3072]{0:T(1024)S(1)}, f32[3072,1024]{0,1:T(8,128)}) fusion(f32[3072,1024]{0,1:T(8,128)} %copy-done.4, f32[3072]{0:T(1024)S(1)} %add_sqrt_fusion, f32[768,1024]{1,0:T(8,128)S(1)} %copy-done.3, f32[768]{0:T(1024)S(1)} %add_sqrt_fusion.1, f32[768,3072]{1,0:T(8,128)} %get-tuple-element.13, f32[768]{0:T(1024)S(1)} %get-tuple-element.3, ...), kind=kOutput, calls=%fused_computation.1 | convolution fusion | flops 4864865280 | bytes 37785600 | tf_op jit(solution)/shard_map/dot_general | solution.py:61
  110.8 0.0 copy-done.2
  110.8 3.9 convolution_bitcast_fusion
  114.7 2.4 copy.13
  117.1 2.9 reshape.35
  120.0 4.2 copy.14
  124.3 0.0 reduce-scatter.3.cloned.1.call-update
  124.3 0.0 reduce-scatter.5.cloned.1.call-start
  124.3 12.6 %fusion.9 = f32[768,1024]{0,1:T(8,128)S(1)} fusion(bf16[1,3072,768]{2,1,0:T(8,128)(2,1)} %all-gather.3.cloned.1.call-done, f32[3072,1024]{0,1:T(8,128)} %get-tuple-element.17, f32[3072]{0:T(1024)S(1)} %get-tuple-element.16, f32[3072]{0:T(1024)S(1)} %add_sqrt_fusion, f32[3072,1024]{0,1:T(8,128)} %copy-done.4), kind=kOutput, calls=%fused_computation.20 | convolution fusion | flops 4850712576 | bytes 33054720 | tf_op jit(solution)/shard_map/dot_general | solution.py:69
  136.9 2.4 copy.15
  139.3 0.0 copy-start.1
  139.3 5.3 reshape.37
  144.6 4.2 copy.16
  148.7 0.0 reduce-scatter.5.cloned.1.call-update
  148.8 0.6 multiply_reduce_fusion.4
  149.4 64.6 %all-reduce = (f32[]{:T(128)}, f32[]{:T(128)}) all-reduce(f32[]{:T(128)} %multiply_reduce_fusion.4, f32[]{:T(128)} %get-tuple-element.5), channel_id=1, replica_groups=mesh['dp'=32,'blk'=4] {'dp','blk'}, use_global_device_ids=true, to_apply=%region_5.6 | all-reduce | flops 2 | bytes 16 | tf_op jit(solution)/shard_map/psum | solution.py:58
  215.4 119.1 %reduce-scatter.3.cloned.1.call-done = f32[24,256]{1,0:T(8,128)} async-done(((f32[3072,256]{1,0:T(8,128)}), f32[24,256]{1,0:T(8,128)}) %reduce-scatter.3.cloned.1.call-update) | async-done | bytes 24592 | tf_op jit(solution)/shard_map/reduce_scatter | solution.py:72
  334.5 2.0 broadcast_divide_fusion.3
  336.5 209.9 %reduce-scatter.5.cloned.1.call-done = f32[24,256]{1,0:T(8,128)} async-done(((f32[3072,256]{1,0:T(8,128)}), f32[24,256]{1,0:T(8,128)}) %reduce-scatter.5.cloned.1.call-update) | async-done | bytes 24592 | tf_op jit(solution)/shard_map/reduce_scatter | solution.py:75
  546.4 2.0 broadcast_divide_fusion.2
  548.4 0.0 copy-done.1
  (2 shorter events, 0.0 us)
Async XLA Ops:
  7.2 57.9 %copy-start = (bf16[768,1024]{1,0:T(8,128)(2,1)S(1)}, bf16[768,1024]{1,0:T(8,128)(2,1)}, u32[]{:S(2)}) copy-start(bf16[768,1024]{1,0:T(8,128)(2,1)} %param.11) | copy-start | bytes 4718596
  7.2 57.8 %all-gather.3.cloned.1.call-start = ((), (), s32[]{:S(2)}) async-start(), calls=%async_computation.4 | async-start | bytes 5898240 | tf_op jit(solution)/shard_map/all_gather | solution.py:48
  7.9 326.6 %reduce-scatter.3.cloned.1.call-start = ((), (), s32[]{:S(2)}) async-start(), calls=%async_computation.2 | async-start | bytes 3170304 | tf_op jit(solution)/shard_map/reduce_scatter | solution.py:72
  65.0 7.4 %copy-start.3 = (f32[768,1024]{1,0:T(8,128)S(1)}, f32[768,1024]{1,0:T(8,128)}, u32[]{:S(2)}) copy-start(f32[768,1024]{1,0:T(8,128)} %get-tuple-element.10) | copy-start | bytes 9437188
  72.4 9.8 %copy-start.4 = (f32[3072,1024]{0,1:T(8,128)}, f32[3072,1024]{0,1:T(8,128)S(1)}, u32[]{:S(2)}) copy-start(f32[3072,1024]{0,1:T(8,128)S(1)} %get-tuple-element.12) | copy-start | bytes 37748740
  95.7 15.1 %copy-start.2 = (bf16[1,768,768]{2,1,0:T(8,128)(2,1)S(1)}, bf16[1,768,768]{2,1,0:T(8,128)(2,1)}, u32[]{:S(2)}) copy-start(bf16[1,768,768]{2,1,0:T(8,128)(2,1)} %param.6) | copy-start | bytes 3538948
  124.3 422.1 %reduce-scatter.5.cloned.1.call-start = ((), (), s32[]{:S(2)}) async-start(), calls=%async_computation.3 | async-start | bytes 3170304 | tf_op jit(solution)/shard_map/reduce_scatter | solution.py:75
  139.3 409.2 %copy-start.1 = (bf16[768,1024]{1,0:T(8,128)(2,1)S(1)}, bf16[768,1024]{1,0:T(8,128)(2,1)}, u32[]{:S(2)}) copy-start(bf16[768,1024]{1,0:T(8,128)(2,1)} %param.11) | copy-start | bytes 4718596
Sparse Core Ops, SparseCore 0:
  9.7 55.3 all-gather.2
  124.4 210.0 reduce-scatter.2
  339.3 207.0 reduce-scatter.4
where the time goes:
time: 557 us; the launch traced here: 556 us
  waiting for transfers between devices  380 us (68%)
  matrix products  67 us (12%)
  blocking collectives  64.6 us (12%)
  local copies, waits for them, and re-layouts  21.4 us (4%)
  between operations  16.3 us (3%)
  other arithmetic  6.71 us (1%)
    reduce_scatter x1, waiting for transfers between devices, per_device(): lax.psum_scatter(spread_blocks(head_prec, dp_size, blk_size), ('dp', 'blk...  210 us
    reduce_scatter x1, waiting for transfers between devices, per_device(): lax.psum_scatter(spread_blocks(head_prod, dp_size, blk_size), ('dp', 'blk...  119 us
    psum x1, blocking collectives, per_device(): loss_sum, weight_total = lax.psum((loss_local, weight_local), ('dp', 'blk'))  64.6 us
    all_gather x1, waiting for transfers between devices, per_device(): feat_prec_all = lax.all_gather(feat_prec, 'blk', axis=0, tiled=True)  50.2 us
    dot_general x1, matrix products, per_device(): lax.dot_general(coeffs, unit16_prod, (((0,), (0,)), ((), ())), preferred_...  15.1 us
    dot_general x1, matrix products, per_device(): jnp.dot(coeffs, unit16_prec, preferred_element_type=jnp.float32)  13.6 us
    dot_general x1, matrix products, per_device(): lax.dot_general(feat_prec_all, dir_prec, (((0,), (0,)), ((), ())), prefer...  12.6 us
    dot_general x2, matrix products, embed_rows(): jnp.dot(features, weight, preferred_element_type=jnp.float32)  12.2 us
  transfers between devices with their start and end apart: 3, of which 3 were waited for; matrix products, arithmetic and copies ran while one was open for 6% of the time, Pallas kernels for 0%

commit v1 on v0

--- a/solution.py
+++ b/solution.py
@@ -45,7 +45,9 @@
     dp_size = lax.axis_size("dp")
     blk_size = lax.axis_size("blk")
     unit_prod, unit16_prod, radius_prod = embed_rows(feat_prod, proj_prod)
-    feat_prec_all = lax.all_gather(feat_prec, "blk", axis=0, tiled=True)
+    feat_prec_all = jnp.concatenate(
+        lax.all_to_all(jnp.stack([feat_prec] * lax.axis_size("blk")), "blk", 0, 0), axis=0
+    )
     unit_prec, unit16_prec, radius_prec = embed_rows(feat_prec_all, proj_prec)
     scores = similarity(unit16_prod, unit16_prec)
     columns = lax.iota(jnp.int32, unit16_prec.shape[0])

time: 557 us -> 566 us (1.016)
  local copies, waits for them, and re-layouts: 21.4 us -> 29.9 us
    all_gather x1 -> x0, waiting for transfers between devices: 50.2 us -> none  [per_device(): feat_prec_all = lax.all_gather(feat_prec, 'blk', axis=0, tiled=True)]
    all_to_all x0 -> x1, waiting for transfers between devices: none -> 50.2 us  [per_device(): lax.all_to_all(jnp.stack([feat_prec] * lax.axis_size('blk')), 'blk', 0, 0)]
where the time goes in v1:
time: 566 us; the launch traced here: 565 us
  waiting for transfers between devices  376 us (66%)
  matrix products  67.6 us (12%)
  blocking collectives  64.9 us (11%)
  local copies, waits for them, and re-layouts  29.9 us (5%)
  between operations  16.6 us (3%)
    reduce_scatter x1, waiting for transfers between devices, per_device(): lax.psum_scatter(spread_blocks(head_prec, dp_size, blk_size), ('dp', 'blk...  210 us
    reduce_scatter x1, waiting for transfers between devices, per_device(): lax.psum_scatter(spread_blocks(head_prod, dp_size, blk_size), ('dp', 'blk...  116 us
    psum x1, blocking collectives, per_device(): loss_sum, weight_total = lax.psum((loss_local, weight_local), ('dp', 'blk'))  64.9 us
    all_to_all x1, waiting for transfers between devices, per_device(): lax.all_to_all(jnp.stack([feat_prec] * lax.axis_size('blk')), 'blk', 0, 0)  50.2 us
    dot_general x1, matrix products, per_device(): lax.dot_general(coeffs, unit16_prod, (((0,), (0,)), ((), ())), preferred_...  15.1 us
    dot_general x1, matrix products, per_device(): lax.dot_general(feat_prec_all, dir_prec, (((0,), (0,)), ((), ())), prefer...  13.7 us
    dot_general x1, matrix products, per_device(): jnp.dot(coeffs, unit16_prec, preferred_element_type=jnp.float32)  13.6 us
    dot_general x2, matrix products, embed_rows(): jnp.dot(features, weight, preferred_element_type=jnp.float32)  11.7 us
  transfers between devices with their start and end apart: 3, of which 3 were waited for; matrix products, arithmetic and copies ran while one was open for 6% of the time, Pallas kernels for 0%

profile of v1, /device:TPU:0, one launch (start us, length us, event | category | flops | bytes accessed | tf_op | source)
XLA Modules:
  0.0 565.3 jit_solution(15258442012262144938)
XLA Ops:
  7.2 0.0 copy-start
  7.2 0.0 copy-start.2
  7.2 0.0 copy-start.3
  7.2 0.0 copy-start.4
  7.2 3.8 stack.3
  11.1 5.4 all-to-all-start
  16.5 0.0 reduce-scatter.3.cloned.1.call-start
  16.5 0.0 copy-done.2
  16.5 0.0 copy-done.3
  16.5 0.6 fusion.15
  17.1 0.0 copy-done.4
  17.1 4.3 multiply_reduce_fusion.3
  21.4 50.2 %all-to-all-done = bf16[4,768,768]{2,1,0:T(8,128)(2,1)} async-done(((bf16[4,768,768]{2,1,0:T(8,128)(2,1)}), bf16[4,768,768]{2,1,0:T(8,128)(2,1)}, u32[]{:S(2)}, u32[]{:S(2)}) %all-to-all-start) | async-done | bytes 4718624 | tf_op jit(solution)/shard_map/all_to_all | solution.py:49
  71.7 0.0 copy-done
  71.7 0.0 copy-start.6
  71.7 7.4 %multiply_reduce_fusion.1 = (f32[3072]{0:T(1024)S(1)}, f32[3072,1024]{0,1:T(8,128)S(1)}) fusion(bf16[3072,768]{1,0:T(8,128)(2,1)} %bitcast.2, bf16[768,1024]{1,0:T(8,128)(2,1)S(1)} %copy-done), kind=kOutput, calls=%fused_computation.2 | convolution fusion | flops 4838126592 | bytes 18886656 | tf_op jit(solution)/shard_map/dot_general | solution.py:11
  79.0 0.0 copy-start.7
  79.1 0.0 copy-done.6
  79.1 9.7 %fusion = (f32[768]{0:T(1024)S(1)}, f32[768]{0:T(1024)S(1)}, f32[768,3072]{1,0:T(8,128)}) fusion(s32[768]{0:T(1024)S(1)} %reduce.2, f32[3072,1024]{0,1:T(8,128)S(1)} %get-tuple-element.12, f32[3072]{0:T(1024)S(1)} %add_sqrt_fusion, f32[768,1024]{1,0:T(8,128)S(1)} %copy-done.6, f32[768]{0:T(1024)S(1)} %add_sqrt_fusion.1), kind=kOutput, calls=%fused_computation.7 | convolution fusion | flops 4853856256 | bytes 25190400 | tf_op jit(solution)/shard_map/dot_general | solution.py:18
  88.8 0.0 copy-done.7
  88.8 13.6 %multiply_reduce_fusion.2 = (f32[768]{0:T(1024)S(1)}, f32[768,1024]{1,0:T(8,128)S(1)}) fusion(f32[768,1024]{1,0:T(8,128)S(1)} %copy-done.6, f32[768]{0:T(1024)S(1)} %add_sqrt_fusion.1, f32[3072,1024]{0,1:T(8,128)} %copy-done.7, f32[3072]{0:T(1024)S(1)} %add_sqrt_fusion, f32[768,3072]{1,0:T(8,128)} %get-tuple-element.13, f32[768]{0:T(1024)S(1)} %get-tuple-element.3, ...), kind=kOutput, calls=%fused_computation.11 | convolution fusion | flops 4860148736 | bytes 28339200 | tf_op jit(solution)/shard_map/dot_general | solution.py:62
  102.3 0.0 copy-start.5
  102.3 15.1 %multiply_reduce_fusion = (f32[3072]{0:T(1024)S(1)}, f32[3072,1024]{0,1:T(8,128)}) fusion(f32[3072,1024]{0,1:T(8,128)} %copy-done.7, f32[3072]{0:T(1024)S(1)} %add_sqrt_fusion, f32[768,1024]{1,0:T(8,128)S(1)} %copy-done.6, f32[768]{0:T(1024)S(1)} %add_sqrt_fusion.1, f32[768,3072]{1,0:T(8,128)} %get-tuple-element.13, f32[768]{0:T(1024)S(1)} %get-tuple-element.3, ...), kind=kOutput, calls=%fused_computation.1 | convolution fusion | flops 4864865280 | bytes 37785600 | tf_op jit(solution)/shard_map/dot_general | solution.py:63
  117.4 0.0 copy-done.5
  117.4 3.8 convolution_bitcast_fusion
  121.3 3.6 copy.13
  124.9 5.1 reshape.40
  130.0 4.2 copy.14
  134.3 0.0 reduce-scatter.3.cloned.1.call-update
  134.3 0.0 reduce-scatter.5.cloned.1.call-start
  134.3 13.7 %fusion.6 = f32[768,1024]{0,1:T(8,128)} fusion(bf16[3072,768]{1,0:T(8,128)(2,1)} %bitcast.2, f32[3072,1024]{0,1:T(8,128)} %get-tuple-element.17, f32[3072]{0:T(1024)S(1)} %get-tuple-element.16, f32[3072]{0:T(1024)S(1)} %add_sqrt_fusion, f32[3072,1024]{0,1:T(8,128)} %copy-done.7), kind=kOutput, calls=%fused_computation.17 | convolution fusion | flops 4850712576 | bytes 33054720 | tf_op jit(solution)/shard_map/dot_general | solution.py:71
  148.0 3.6 copy.15
  151.6 0.0 copy-start.1
  151.6 5.3 reshape.42
  156.9 4.2 copy.16
  161.1 0.0 reduce-scatter.5.cloned.1.call-update
  161.1 0.6 multiply_reduce_fusion.4
  161.7 64.9 %all-reduce = (f32[]{:T(128)}, f32[]{:T(128)}) all-reduce(f32[]{:T(128)} %multiply_reduce_fusion.4, f32[]{:T(128)} %get-tuple-element.5), channel_id=1, replica_groups=mesh['dp'=32,'blk'=4] {'dp','blk'}, use_global_device_ids=true, to_apply=%region_5.6 | all-reduce | flops 2 | bytes 16 | tf_op jit(solution)/shard_map/psum | solution.py:60
  227.9 115.5 %reduce-scatter.3.cloned.1.call-done = f32[24,256]{1,0:T(8,128)} async-done(((f32[3072,256]{1,0:T(8,128)}), f32[24,256]{1,0:T(8,128)}) %reduce-scatter.3.cloned.1.call-update) | async-done | bytes 24592 | tf_op jit(solution)/shard_map/reduce_scatter | solution.py:74
  343.4 2.0 broadcast_divide_fusion.3
  345.4 209.9 %reduce-scatter.5.cloned.1.call-done = f32[24,256]{1,0:T(8,128)} async-done(((f32[3072,256]{1,0:T(8,128)}), f32[24,256]{1,0:T(8,128)}) %reduce-scatter.5.cloned.1.call-update) | async-done | bytes 24592 | tf_op jit(solution)/shard_map/reduce_scatter | solution.py:77
  555.3 2.0 broadcast_divide_fusion.2
  557.3 0.0 copy-done.1
  (3 shorter events, 0.0 us)
Async XLA Ops:
  7.2 64.5 %copy-start = (bf16[768,1024]{1,0:T(8,128)(2,1)S(1)}, bf16[768,1024]{1,0:T(8,128)(2,1)}, u32[]{:S(2)}) copy-start(bf16[768,1024]{1,0:T(8,128)(2,1)} %param.11) | copy-start | bytes 4718596
  7.2 9.3 %copy-start.2 = (s32[1,768]{1,0:T(1,128)S(1)}, s32[1,768]{1,0:T(1,128)}, u32[]{:S(2)}) copy-start(s32[1,768]{1,0:T(1,128)} %param.8) | copy-start | bytes 9220
  7.2 9.3 %copy-start.3 = (f32[1,768]{1,0:T(1,128)S(1)}, f32[1,768]{1,0:T(1,128)}, u32[]{:S(2)}) copy-start(f32[1,768]{1,0:T(1,128)} %param.9) | copy-start | bytes 9220
  7.2 9.9 %copy-start.4 = (bf16[768,1024]{1,0:T(8,128)(2,1)S(1)}, bf16[768,1024]{1,0:T(8,128)(2,1)}, u32[]{:S(2)}) copy-start(bf16[768,1024]{1,0:T(8,128)(2,1)} %param.10) | copy-start | bytes 4718596
  11.1 60.6 %all-to-all-start = ((bf16[4,768,768]{2,1,0:T(8,128)(2,1)}), bf16[4,768,768]{2,1,0:T(8,128)(2,1)}, u32[]{:S(2)}, u32[]{:S(2)}) async-start(bf16[4,768,768]{2,1,0:T(8,128)(2,1)} %stack.3), calls=%async_computation | async-start | bytes 9437184 | tf_op jit(solution)/shard_map/all_to_all | solution.py:49
  16.5 327.0 %reduce-scatter.3.cloned.1.call-start = ((), (), s32[]{:S(2)}) async-start(), calls=%async_computation.3 | async-start | bytes 3170304 | tf_op jit(solution)/shard_map/reduce_scatter | solution.py:74
  71.7 7.4 %copy-start.6 = (f32[768,1024]{1,0:T(8,128)S(1)}, f32[768,1024]{1,0:T(8,128)}, u32[]{:S(2)}) copy-start(f32[768,1024]{1,0:T(8,128)} %get-tuple-element.10) | copy-start | bytes 9437188
  79.0 9.7 %copy-start.7 = (f32[3072,1024]{0,1:T(8,128)}, f32[3072,1024]{0,1:T(8,128)S(1)}, u32[]{:S(2)}) copy-start(f32[3072,1024]{0,1:T(8,128)S(1)} %get-tuple-element.12) | copy-start | bytes 37748740
  102.3 15.1 %copy-start.5 = (bf16[1,768,768]{2,1,0:T(8,128)(2,1)S(1)}, bf16[1,768,768]{2,1,0:T(8,128)(2,1)}, u32[]{:S(2)}) copy-start(bf16[1,768,768]{2,1,0:T(8,128)(2,1)} %param.6) | copy-start | bytes 3538948
  134.3 421.0 %reduce-scatter.5.cloned.1.call-start = ((), (), s32[]{:S(2)}) async-start(), calls=%async_computation.4 | async-start | bytes 3170304 | tf_op jit(solution)/shard_map/reduce_scatter | solution.py:77
  151.6 405.7 %copy-start.1 = (bf16[768,1024]{1,0:T(8,128)(2,1)S(1)}, bf16[768,1024]{1,0:T(8,128)(2,1)}, u32[]{:S(2)}) copy-start(bf16[768,1024]{1,0:T(8,128)(2,1)} %param.11) | copy-start | bytes 4718596
Sparse Core Ops, SparseCore 0:
  134.4 208.9 reduce-scatter.2
  348.2 207.0 reduce-scatter.4
